TPU v7x, 32 devices: a whole 2x2x4 slice. The times are simulated.
32 devices in a mesh: dp: 4 (over z), expert: 4 (over y, x), tensor: 2 (over core).
Axes of the slice: x: 2, y: 2, z: 4, core: 2. Of those that a mesh axis runs over, the one named last changes fastest.
Arguments:
- tokens: bfloat16 [2048, 2048], P(('dp', 'expert')), may hold values from -6 to 6
- grad_out: bfloat16 [2048, 2048], P(('dp', 'expert')), may hold values from -6 to 6
- route_ids: int32 [2048, 8], P(('dp', 'expert')), may hold values from 0 to 15, all different within a row; in each aligned block of 128 rows (0 to 127, 128 to 255, ...) at most 72 rows name the same one
- gate_values: bfloat16 [2048, 8], P(('dp', 'expert')), may hold values from 0.049804688 to 0.5
- gate_proj: bfloat16 [16, 2048, 768], P(('dp', 'expert'), None, 'tensor'), may hold values from -0.125 to 0.125
- up_proj: bfloat16 [16, 2048, 768], P(('dp', 'expert'), None, 'tensor'), may hold values from -0.125 to 0.125
- down_proj: bfloat16 [16, 768, 2048], P(('dp', 'expert'), 'tensor'), may hold values from -0.21875 to 0.21875
Outputs:
- token_grad: bfloat16 [2048, 2048], P(('dp', 'expert'), 'tensor')
- gate_grad: bfloat16 [2048, 8], P(('dp', 'expert'))
- gate_proj_grad: bfloat16 [16, 2048, 768], P(('dp', 'expert'), None, 'tensor')
- up_proj_grad: bfloat16 [16, 2048, 768], P(('dp', 'expert'), None, 'tensor')
- down_proj_grad: bfloat16 [16, 768, 2048], P(('dp', 'expert'), 'tensor')
Inputs may be any that keep to these rules, and one draw needn't show every extreme that they name: `route_ids`: each token names 8 different experts. Among the rows of one device (128 tokens), no expert is named more than 72 times, a bound that some block reaches.
All inputs are finite; a program needn't handle non-finite values.
Results may differ from a plain program's by a relative error of at most 0.008.
Values may be sent and summed in bfloat16 or wider, within the bound.
No kernel may reach another device: no remote copies, remote signals or barrier semaphores. Data moves between devices by JAX's collectives and lax.ppermute only.
A program may use at most 128 MiB of HBM per device.

v0:
```python
import jax
import jax.numpy as jnp
from jax import lax
from jax.sharding import PartitionSpec as P


def on_device(tokens, grad_out, route_ids, gate_values, gate_proj, up_proj, down_proj):
    tok_rows, features = tokens.shape
    top_count = route_ids.shape[1]
    n_dp = lax.axis_size("dp")
    n_ex = lax.axis_size("expert")
    groups = n_dp * n_ex
    capacity = max(2, tok_rows * top_count * 9 // (8 * groups))
    plane = lax.axis_index("dp")
    core = lax.axis_index("tensor")
    col_rows = n_dp * tok_rows
    plane_slots = n_dp * capacity
    slots = n_ex * plane_slots
    ids_all = lax.all_gather(route_ids, "dp", tiled=True)
    gates_all = lax.all_gather(gate_values, "dp", tiled=True)
    carried = jnp.where(core == 0, tokens, grad_out)
    carried_all = lax.all_gather(carried, "dp", tiled=True)
    routes = tok_rows * top_count
    ids_blk = ids_all.reshape(n_dp, routes)
    local_ex = ids_blk - plane * n_ex
    in_plane = (local_ex >= 0) & (local_ex < n_ex)
    one_hot = local_ex[:, :, None] == jnp.arange(n_ex, dtype=jnp.int32)[None, None, :]
    one_hot_b = one_hot.astype(jnp.bfloat16)
    r_iota = jnp.arange(routes, dtype=jnp.int32)
    earlier = (r_iota[None, :] < r_iota[:, None]).astype(jnp.bfloat16)
    running = jnp.einsum("ab,nbe->nae", earlier, one_hot_b, preferred_element_type=jnp.float32)
    position = jnp.sum(running * one_hot.astype(jnp.float32), axis=2).astype(jnp.int32)
    blk = jnp.arange(n_dp, dtype=jnp.int32)[:, None]
    slot_of = jnp.where(in_plane, local_ex * plane_slots + blk * capacity + position, -1)
    slot_of = slot_of.reshape(col_rows, top_count)
    s_iota = jnp.arange(slots, dtype=jnp.int32)
    match = slot_of[None, :, :] == s_iota[:, None, None]
    select = jnp.sum(match.astype(jnp.bfloat16), axis=2)
    send = jnp.dot(select, carried_all, preferred_element_type=jnp.float32).astype(tokens.dtype)
    send_gate = jnp.sum(
        jnp.where(match, gates_all.astype(jnp.float32)[None, :, :], 0.0), axis=(1, 2)
    ).astype(gate_values.dtype)
    recv = lax.all_to_all(send, "expert", split_axis=0, concat_axis=0, tiled=True)
    routed_gate = lax.all_to_all(send_gate, "expert", split_axis=0, concat_axis=0, tiled=True)
    both = lax.all_gather(recv, "tensor")
    routed_x = both[0]
    routed_dy = both[1]
    weight_g = gate_proj[0]
    weight_u = up_proj[0]
    weight_d = down_proj[0]
    gate_pre = jnp.dot(routed_x, weight_g, preferred_element_type=jnp.float32)
    up_pre = jnp.dot(routed_x, weight_u, preferred_element_type=jnp.float32)
    sig_gate = jax.nn.sigmoid(gate_pre)
    silu_gate = gate_pre * sig_gate
    activation = (silu_gate * up_pre).astype(jnp.bfloat16)
    hidden_grad = lax.dot_general(
        routed_dy, weight_d, (((1,), (1,)), ((), ())), preferred_element_type=jnp.float32
    )
    gate_terms = jnp.sum(hidden_grad * activation.astype(jnp.float32), axis=1)
    row_gate = routed_gate.astype(jnp.float32)[:, None]
    scaled = row_gate * hidden_grad
    up_grad = (scaled * silu_gate).astype(jnp.bfloat16)
    pre_grad = (scaled * up_pre * sig_gate * (1.0 + gate_pre * (1.0 - sig_gate))).astype(
        jnp.bfloat16
    )
    grad_g = lax.dot_general(
        routed_x, pre_grad, (((0,), (0,)), ((), ())), preferred_element_type=jnp.float32
    ).astype(jnp.bfloat16)
    grad_u = lax.dot_general(
        routed_x, up_grad, (((0,), (0,)), ((), ())), preferred_element_type=jnp.float32
    ).astype(jnp.bfloat16)
    weighted = (row_gate * activation.astype(jnp.float32)).astype(jnp.bfloat16)
    grad_d = lax.dot_general(
        weighted, routed_dy, (((0,), (0,)), ((), ())), preferred_element_type=jnp.float32
    ).astype(jnp.bfloat16)
    partial_value = lax.dot_general(
        pre_grad, weight_g, (((1,), (1,)), ((), ())), preferred_element_type=jnp.float32
    ) + lax.dot_general(
        up_grad, weight_u, (((1,), (1,)), ((), ())), preferred_element_type=jnp.float32
    )
    routed_grad = lax.psum_scatter(partial_value, "tensor", scatter_dimension=1, tiled=True).astype(
        jnp.bfloat16
    )
    slot_gate = lax.psum(gate_terms, "tensor").astype(jnp.bfloat16)
    back_rows = lax.all_to_all(routed_grad, "expert", split_axis=0, concat_axis=0, tiled=True)
    back_gate = lax.all_to_all(slot_gate, "expert", split_axis=0, concat_axis=0, tiled=True)
    col_grad = lax.dot_general(
        select, back_rows, (((0,), (0,)), ((), ())), preferred_element_type=jnp.float32
    )
    token_grad = lax.psum_scatter(col_grad, "dp", scatter_dimension=0, tiled=True).astype(
        jnp.bfloat16
    )
    col_gate = jnp.sum(jnp.where(match, back_gate.astype(jnp.float32)[:, None, None], 0.0), axis=0)
    gate_grad = lax.psum_scatter(col_gate, "dp", scatter_dimension=0, tiled=True).astype(
        jnp.bfloat16
    )
    return (token_grad, gate_grad, grad_g[None], grad_u[None], grad_d[None])


def solution(mesh):
    in_specs = (
        P(("dp", "expert"), None),
        P(("dp", "expert"), None),
        P(("dp", "expert"), None),
        P(("dp", "expert"), None),
        P(("dp", "expert"), None, "tensor"),
        P(("dp", "expert"), None, "tensor"),
        P(("dp", "expert"), "tensor", None),
    )
    out_specs = (
        P(("dp", "expert"), "tensor"),
        P(("dp", "expert"), None),
        P(("dp", "expert"), None, "tensor"),
        P(("dp", "expert"), None, "tensor"),
        P(("dp", "expert"), "tensor", None),
    )
    return jax.shard_map(
        on_device, mesh=mesh, in_specs=in_specs, out_specs=out_specs, check_vma=False
    )
```

profile of v0, /device:TPU:0, one launch (start us, length us, event | category | flops | bytes accessed | tf_op | source)
XLA Modules:
  0.0 313.8 jit_solution(6951644346922703783)
XLA Ops:
  9.4 16.3 %all_gather.15 = s32[512,8]{1,0:T(8,128)S(1)} all-gather(s32[128,8]{1,0:T(8,128)S(1)} %copy.20), channel_id=1, replica_groups=mesh['dp'=4,'expert'=4,'tensor'=2] {'dp'}, dimensions={0}, use_global_device_ids=true | all-gather | bytes 20480 | tf_op jit(solution)/shard_map/all_gather | solution.py:19
  26.9 12.2 %fusion.1 = bf16[1152,512]{1,0:T(8,128)(2,1)S(1)} fusion(s32[512,8]{0,1:T(8,128)S(1)} %copy.21), kind=kLoop, calls=%fused_computation.5 | loop fusion | flops 13565952 | bytes 1196032 | tf_op jit(solution)/shard_map/reduce_sum | solution.py:38
  39.1 20.3 %all-gather.3.cloned.1.call-done = bf16[512,2048]{1,0:T(8,128)(2,1)} async-done(((bf16[128,2048]{1,0:T(8,128)(2,1)}), bf16[512,2048]{1,0:T(8,128)(2,1)}) %all-gather.3.cloned.1.call-update) | async-done | bytes 2097168 | tf_op jit(solution)/shard_map/all_gather | solution.py:22
  59.4 4.4 %convolution_convert_fusion = bf16[1152,2048]{1,0:T(8,128)(2,1)S(1)} fusion(bf16[1152,512]{1,0:T(8,128)(2,1)S(1)} %fusion.1, bf16[512,2048]{1,0:T(8,128)(2,1)} %all-gather.3.cloned.1.call-done), kind=kOutput, calls=%fused_computation.6 | convolution fusion | flops 2418278400 | bytes 7995392 | tf_op jit(solution)/shard_map/dot_general | solution.py:39
  63.9 57.6 %all_to_all.37 = bf16[4,288,2048]{2,1,0:T(8,128)(2,1)} all-to-all(bf16[4,288,2048]{2,1,0:T(8,128)(2,1)S(1)} %bitcast.82), channel_id=1, replica_groups=mesh['dp'=4,'expert'=4,'tensor'=2] {'expert'}, dimensions={0} | all-to-all | bytes 9437184 | tf_op jit(solution)/shard_map/all_to_all | solution.py:43
  121.5 18.9 %all-gather.5.cloned.1.call-done = bf16[2,1152,2048]{2,1,0:T(8,128)(2,1)} async-done(((bf16[1,1152,2048]{2,1,0:T(8,128)(2,1)}), bf16[2,1152,2048]{2,1,0:T(8,128)(2,1)}) %all-gather.5.cloned.1.call-update) | async-done | bytes 9437200 | tf_op jit(solution)/shard_map/all_gather | solution.py:45
  140.4 4.8 %fusion.9 = f32[1152,384]{0,1:T(8,128)S(1)} fusion(bf16[2,1152,2048]{2,1,0:T(8,128)(2,1)} %all-gather.5.cloned.1.call-done, bf16[1,2048,384]{2,1,0:T(8,128)(2,1)S(1)} %copy-done), kind=kOutput, calls=%fused_computation.16 | convolution fusion | flops 1811939328 | bytes 8060928 | tf_op jit(solution)/shard_map/dot_general | solution.py:51
  147.9 3.8 %fusion.17 = (f32[1152]{0:T(1024)S(1)}, bf16[1152,384]{0,1:T(8,128)(2,1)}, f32[1152,384]{0,1:T(8,128)}) fusion(f32[1152,384]{0,1:T(8,128)S(1)} %fusion.10, f32[1152,384]{0,1:T(8,128)S(1)} %fusion.9, bf16[1,384,2048]{2,1,0:T(8,128)(2,1)S(1)} %copy-done.12, bf16[2,1152,2048]{2,1,0:T(8,128)(2,1)S(1)} %copy-done.11), kind=kOutput, calls=%fused_computation.26 | convolution fusion | flops 1815919488 | bytes 12489216 | tf_op jit(solution)/shard_map/dot_general | solution.py:56
  156.2 3.9 %all-to-all-start.3 = ((bf16[4,2,144]{2,1,0:T(2,128)(2,1)}), bf16[4,2,144]{2,1,0:T(2,128)(2,1)S(1)}, u32[]{:S(2)}, u32[]{:S(2)}) async-start(bf16[4,2,144]{2,1,0:T(2,128)(2,1)} %reshape.85), calls=%async_computation.5 | async-start | bytes 8192 | tf_op jit(solution)/shard_map/all_to_all | solution.py:86
  160.1 11.9 %all_gather.16 = bf16[512,8]{0,1:T(8,128)(2,1)S(1)} all-gather(bf16[128,8]{0,1:T(8,128)(2,1)S(1)} %copy-done.10), channel_id=1, replica_groups=mesh['dp'=4,'expert'=4,'tensor'=2] {'dp'}, dimensions={0}, use_global_device_ids=true | all-gather | bytes 10240 | tf_op jit(solution)/shard_map/all_gather | solution.py:20
  172.3 11.9 %select_reduce_fusion = (f32[512,8]{0,1:T(8,128)}, bf16[1152]{0:T(1024)(128)(2,1)S(1)}) fusion(f32[1152]{0:T(1024)S(1)} %reshape.81, s32[512,8]{0,1:T(8,128)S(1)} %copy.21, f32[512,8]{0,1:T(8,128)S(1)} %convert_element_type.95), kind=kLoop, calls=%fused_computation | loop fusion | flops 23587712 | bytes 56064 | tf_op jit(solution)/shard_map/reduce_sum | solution.py:93
  185.0 8.6 %all_to_all.38 = bf16[4,2,144]{2,1,0:T(2,128)(2,1)S(1)} all-to-all(bf16[4,2,144]{2,1,0:T(2,128)(2,1)S(1)} %reshape.87), channel_id=1, replica_groups=mesh['dp'=4,'expert'=4,'tensor'=2] {'expert'}, dimensions={0} | all-to-all | bytes 4608 | tf_op jit(solution)/shard_map/all_to_all | solution.py:44
  193.9 3.4 %multiply_convert_fusion.1 = (bf16[1152,384]{0,1:T(8,128)(2,1)S(1)}, bf16[1152,384]{0,1:T(8,128)(2,1)S(1)}) fusion(f32[1152,384]{0,1:T(8,128)} %get-tuple-element.11, f32[1152]{0:T(1024)S(1)} %reshape.80, f32[1152,384]{0,1:T(8,128)} %copy-done.5, f32[1152,384]{0,1:T(8,128)} %copy-done.6), kind=kLoop, calls=%fused_computation.29 | loop fusion | flops 6193152 | bytes 7082496 | tf_op jit(solution)/shard_map/convert_element_type | solution.py:62
  197.3 2.7 fusion.20
  200.0 5.1 %convolution_add_fusion = f32[1152,2048]{1,0:T(8,128)} fusion(f32[1152,2048]{1,0:T(8,128)S(1)} %fusion.20, bf16[1152,384]{0,1:T(8,128)(2,1)S(1)} %get-tuple-element.9, bf16[1,2048,384]{2,1,0:T(8,128)(2,1)S(1)} %copy-done.8), kind=kOutput, calls=%fused_computation.4 | convolution fusion | flops 1814298624 | bytes 21331968 | tf_op jit(solution)/shard_map/dot_general | solution.py:78
  205.2 15.8 %reduce-scatter.4.cloned.1.call-done = f32[1152,1024]{1,0:T(8,128)} async-done(((f32[1152,2048]{1,0:T(8,128)}), f32[1152,1024]{1,0:T(8,128)}) %reduce-scatter.4.cloned.1.call-update) | async-done | bytes 4718608 | tf_op jit(solution)/shard_map/reduce_scatter | solution.py:81
  221.0 4.1 %convert_element_type.103 = bf16[1152,1024]{1,0:T(8,128)(2,1)} convert(f32[1152,1024]{1,0:T(8,128)} %reduce-scatter.4.cloned.1.call-done) | non-fusion elementwise | flops 1179648 | bytes 7077888 | tf_op jit(solution)/shard_map/convert_element_type | solution.py:81
  225.1 4.0 %all-to-all-start.2 = ((bf16[4,288,1024]{2,1,0:T(8,128)(2,1)}), bf16[4,288,1024]{2,1,0:T(8,128)(2,1)S(1)}, u32[]{:S(2)}, u32[]{:S(2)}) async-start(bf16[4,288,1024]{2,1,0:T(8,128)(2,1)} %bitcast.10), calls=%async_computation.3 | async-start | bytes 4718592 | tf_op jit(solution)/shard_map/all_to_all | solution.py:85
  230.0 27.1 %all-to-all-done.2 = bf16[4,288,1024]{2,1,0:T(8,128)(2,1)S(1)} async-done(((bf16[4,288,1024]{2,1,0:T(8,128)(2,1)}), bf16[4,288,1024]{2,1,0:T(8,128)(2,1)S(1)}, u32[]{:S(2)}, u32[]{:S(2)}) %all-to-all-start.2) | async-done | bytes 2359328 | tf_op jit(solution)/shard_map/all_to_all | solution.py:85
  257.1 4.1 %fusion.38 = f32[512,1024]{1,0:T(8,128)} fusion(bf16[1152,512]{1,0:T(8,128)(2,1)} %copy-done.2, bf16[1152,1024]{1,0:T(8,128)(2,1)S(1)} %bitcast.81), kind=kOutput, calls=%fused_computation.52 | convolution fusion | flops 1207959552 | bytes 5636096 | tf_op jit(solution)/shard_map/dot_general | solution.py:87
  262.4 5.8 %fusion.14 = bf16[1,384,2048]{2,1,0:T(8,128)(2,1)} fusion(bf16[2,1152,2048]{2,1,0:T(8,128)(2,1)} %all-gather.5.cloned.1.call-done, bf16[1152,384]{0,1:T(8,128)(2,1)S(1)} %copy-done.13, f32[1152]{0:T(1024)S(1)} %reshape.80), kind=kOutput, calls=%fused_computation.21 | convolution fusion | flops 1814052864 | bytes 7180800 | tf_op jit(solution)/shard_map/dot_general | solution.py:73
  268.2 6.4 %fusion.15 = bf16[1,2048,384]{2,1,0:T(8,128)(2,1)} fusion(bf16[1152,384]{0,1:T(8,128)(2,1)S(1)} %get-tuple-element.9, bf16[2,1152,2048]{2,1,0:T(8,128)(2,1)} %all-gather.5.cloned.1.call-done), kind=kOutput, calls=%fused_computation.22 | convolution fusion | flops 1812725760 | bytes 7176192 | tf_op jit(solution)/shard_map/dot_general | solution.py:69
  274.7 3.9 %fusion.16 = bf16[1,2048,384]{2,1,0:T(8,128)(2,1)} fusion(bf16[1152,384]{0,1:T(8,128)(2,1)S(1)} %copy-done.4, bf16[2,1152,2048]{2,1,0:T(8,128)(2,1)S(1)} %bitcast.86), kind=kOutput, calls=%fused_computation.23 | convolution fusion | flops 1812725760 | bytes 7176192 | tf_op jit(solution)/shard_map/dot_general | solution.py:66
  279.9 25.6 %reduce-scatter.6.cloned.1.call-done = f32[128,1024]{1,0:T(8,128)} async-done(((f32[512,1024]{1,0:T(8,128)}), f32[128,1024]{1,0:T(8,128)}) %reduce-scatter.6.cloned.1.call-update) | async-done | bytes 524304 | tf_op jit(solution)/shard_map/reduce_scatter | solution.py:90
  (76 shorter events, 16.9 us)
Async XLA Ops:
  7.2 133.2 %copy-start = (bf16[1,2048,384]{2,1,0:T(8,128)(2,1)S(1)}, bf16[1,2048,384]{2,1,0:T(8,128)(2,1)}, u32[]{:S(2)}) copy-start(bf16[1,2048,384]{2,1,0:T(8,128)(2,1)} %param.11) | copy-start | bytes 4718596
  7.2 2.1 copy-start.9
  7.2 52.2 %all-gather.3.cloned.1.call-start = ((), (), s32[]{:S(2)}) async-start(), calls=%async_computation.7 | async-start | bytes 2621440 | tf_op jit(solution)/shard_map/all_gather | solution.py:22
  9.3 131.1 %all-gather.5.cloned.1.call-start = ((), (), s32[]{:S(2)}) async-start(), calls=%async_computation.8 | async-start | bytes 14155776 | tf_op jit(solution)/shard_map/all_gather | solution.py:45
  39.1 24.7 %copy-start.2 = (bf16[1152,512]{1,0:T(8,128)(2,1)}, bf16[1152,512]{1,0:T(8,128)(2,1)S(1)}, u32[]{:S(2)}) copy-start(bf16[1152,512]{1,0:T(8,128)(2,1)S(1)} %fusion.1) | copy-start | bytes 3538948
  121.5 23.7 %copy-start.7 = (bf16[1,2048,384]{2,1,0:T(8,128)(2,1)S(1)}, bf16[1,2048,384]{2,1,0:T(8,128)(2,1)}, u32[]{:S(2)}) copy-start(bf16[1,2048,384]{2,1,0:T(8,128)(2,1)} %param.12) | copy-start | bytes 4718596
  140.4 5.1 %copy-start.11 = (bf16[2,1152,2048]{2,1,0:T(8,128)(2,1)S(1)}, bf16[2,1152,2048]{2,1,0:T(8,128)(2,1)}, u32[]{:S(2)}) copy-start(bf16[2,1152,2048]{2,1,0:T(8,128)(2,1)} %all-gather.5.cloned.1.call-done) | copy-start | bytes 28311556
  145.5 2.4 copy-start.5
  145.5 2.4 copy-start.12
  147.9 3.9 %copy-start.6 = (f32[1152,384]{0,1:T(8,128)}, f32[1152,384]{0,1:T(8,128)S(1)}, u32[]{:S(2)}) copy-start(f32[1152,384]{0,1:T(8,128)S(1)} %fusion.10) | copy-start | bytes 5308420
  147.9 12.2 %copy-start.10 = (bf16[128,8]{0,1:T(8,128)(2,1)S(1)}, bf16[128,8]{0,1:T(8,128)(2,1)}, u32[]{:S(2)}) copy-start(bf16[128,8]{0,1:T(8,128)(2,1)} %param.10) | copy-start | bytes 6148
  156.2 15.8 %all-to-all-start.3 = ((bf16[4,2,144]{2,1,0:T(2,128)(2,1)}), bf16[4,2,144]{2,1,0:T(2,128)(2,1)S(1)}, u32[]{:S(2)}, u32[]{:S(2)}) async-start(bf16[4,2,144]{2,1,0:T(2,128)(2,1)} %reshape.85), calls=%async_computation.5 | async-start | bytes 8192 | tf_op jit(solution)/shard_map/all_to_all | solution.py:86
  160.1 60.9 %reduce-scatter.4.cloned.1.call-start = ((), (), s32[]{:S(2)}) async-start(), calls=%async_computation.9 | async-start | bytes 14155776 | tf_op jit(solution)/shard_map/reduce_scatter | solution.py:81
  197.3 2.7 copy-start.3
  197.3 2.7 copy-start.8
  225.1 32.0 %all-to-all-start.2 = ((bf16[4,288,1024]{2,1,0:T(8,128)(2,1)}), bf16[4,288,1024]{2,1,0:T(8,128)(2,1)S(1)}, u32[]{:S(2)}, u32[]{:S(2)}) async-start(bf16[4,288,1024]{2,1,0:T(8,128)(2,1)} %bitcast.10), calls=%async_computation.3 | async-start | bytes 4718592 | tf_op jit(solution)/shard_map/all_to_all | solution.py:85
  229.1 49.5 %reduce-scatter.8.cloned.1.call-start = ((), (), s32[]{:S(2)}) async-start(), calls=%async_computation.11 | async-start | bytes 20480 | tf_op jit(solution)/shard_map/reduce_scatter | solution.py:94
  229.7 75.8 %reduce-scatter.6.cloned.1.call-start = ((), (), s32[]{:S(2)}) async-start(), calls=%async_computation.10 | async-start | bytes 2621440 | tf_op jit(solution)/shard_map/reduce_scatter | solution.py:90
  261.2 1.2 copy-start.13
  262.4 12.3 %slice-start = ((s8[9437184]{0:T(1024)(128)(4,1)}), s8[4194304]{0:T(1024)(128)(4,1)S(1)}, s32[]{:S(2)}) async-start(s8[9437184]{0:T(1024)(128)(4,1)} %bitcast.85), calls=%async_computation.12 | async-start | bytes 8388608
  262.4 12.3 %slice-start.1 = ((s8[9437184]{0:T(1024)(128)(4,1)}), s8[4194304]{0:T(1024)(128)(4,1)S(1)}, s32[]{:S(2)}) async-start(s8[9437184]{0:T(1024)(128)(4,1)} %bitcast.85), calls=%async_computation.13 | async-start | bytes 8388608
  268.2 6.4 %copy-start.4 = (bf16[1152,384]{0,1:T(8,128)(2,1)S(1)}, bf16[1152,384]{0,1:T(8,128)(2,1)}, u32[]{:S(2)}) copy-start(bf16[1152,384]{0,1:T(8,128)(2,1)} %copy-done.3) | copy-start | bytes 2654212
  268.2 6.4 %slice-start.2 = ((s8[9437184]{0:T(1024)(128)(4,1)}), s8[1048576]{0:T(1024)(128)(4,1)S(1)}, s32[]{:S(2)}) async-start(s8[9437184]{0:T(1024)(128)(4,1)} %bitcast.85), calls=%async_computation.14 | async-start | bytes 2097152
  274.7 32.6 %copy-start.1 = (bf16[1,2048,384]{2,1,0:T(8,128)(2,1)S(1)}, bf16[1,2048,384]{2,1,0:T(8,128)(2,1)}, u32[]{:S(2)}) copy-start(bf16[1,2048,384]{2,1,0:T(8,128)(2,1)} %param.11) | copy-start | bytes 4718596
Sparse Core Ops, SparseCore 0:
  10.2 49.2 all-gather.2
  121.6 18.7 all-gather.4
  205.3 15.6 reduce-scatter.3
  232.4 20.2 reduce-scatter.7
  261.4 44.0 reduce-scatter.5
where the time goes:
time: 314 us
  waiting for transfers between devices  108 us (34%)
  blocking collectives  96.9 us (31%)
  matrix products  44 us (14%)
  other arithmetic  38.3 us (12%)
  between operations  14 us (4%)
  starting transfers between devices  8.28 us (3%)
  local copies, waits for them, and re-layouts  3.91 us (1%)
    all_to_all x1, blocking collectives, on_device(): lax.all_to_all(send, 'expert', split_axis=0, concat_axis=0, tiled=True)  57.6 us
    all_to_all x1, waiting for transfers between devices, on_device(): lax.all_to_all(routed_grad, 'expert', split_axis=0, concat_axis=0, tiled=...  27.1 us
    reduce_scatter x1, waiting for transfers between devices, on_device(): lax.psum_scatter(col_grad, 'dp', scatter_dimension=0, tiled=True)  25.6 us
    all_gather x1, waiting for transfers between devices, on_device(): carried_all = lax.all_gather(carried, 'dp', tiled=True)  20.3 us
    all_gather x1, waiting for transfers between devices, on_device(): both = lax.all_gather(recv, 'tensor')  18.9 us
    all_gather x1, blocking collectives, on_device(): ids_all = lax.all_gather(route_ids, 'dp', tiled=True)  16.3 us
    reduce_scatter x1, waiting for transfers between devices, on_device(): lax.psum_scatter(partial_value, 'tensor', scatter_dimension=1, tiled=True)  15.8 us
    reduce_sum x1, other arithmetic, on_device(): select = jnp.sum(match.astype(jnp.bfloat16), axis=2)  12.2 us
  transfers between devices with their start and end apart: 7, of which 5 were waited for; matrix products, arithmetic and copies ran while one was open for 11% of the time, Pallas kernels for 0%

commit v1 on v0

--- a/solution.py
+++ b/solution.py
@@ -17,7 +17,9 @@
     plane_slots = n_dp * capacity
     slots = n_ex * plane_slots
     ids_all = lax.all_gather(route_ids, "dp", tiled=True)
-    gates_all = lax.all_gather(gate_values, "dp", tiled=True)
+    gates_all = jnp.concatenate(
+        lax.all_to_all(jnp.stack([gate_values] * lax.axis_size("dp")), "dp", 0, 0), axis=0
+    )
     carried = jnp.where(core == 0, tokens, grad_out)
     carried_all = lax.all_gather(carried, "dp", tiled=True)
     routes = tok_rows * top_count

time: 314 us -> 307 us (0.978)
  blocking collectives: 96.9 us -> 83.2 us
  starting transfers between devices: 8.28 us -> 11.8 us
    all_gather x1 -> x0, blocking collectives: 11.9 us -> none  [on_device(): gates_all = lax.all_gather(gate_values, 'dp', tiled=True)]
    all_to_all x1, waiting for transfers between devices: 0.01 us -> 4.67 us  [on_device(): lax.all_to_all(slot_gate, 'expert', split_axis=0, concat_axis=0, tiled=True)]
    all_gather x1, waiting for transfers between devices: 18.9 us -> 14.4 us  [on_device(): both = lax.all_gather(recv, 'tensor')]
    all_to_all x0 -> x1, starting transfers between devices: none -> 3.44 us  [on_device(): lax.all_to_all(jnp.stack([gate_values] * lax.axis_size('dp')), 'dp', 0, 0)]
  transfers between devices with their start and end apart: 7 -> 8, of which waited for: 5 -> 6; matrix products, arithmetic and copies ran while one was open for 11% -> 16% of each run, Pallas kernels for 0% -> 0%
where the time goes in v1:
time: 307 us; the launch traced here: 306 us
  waiting for transfers between devices  110 us (36%)
  blocking collectives  83.2 us (27%)
  matrix products  44 us (14%)
  other arithmetic  38.3 us (12%)
  between operations  14 us (5%)
  starting transfers between devices  11.8 us (4%)
  local copies, waits for them, and re-layouts  5.16 us (2%)
    all_to_all x1, blocking collectives, on_device(): lax.all_to_all(send, 'expert', split_axis=0, concat_axis=0, tiled=True)  57.4 us
    all_to_all x1, waiting for transfers between devices, on_device(): lax.all_to_all(routed_grad, 'expert', split_axis=0, concat_axis=0, tiled=...  27.2 us
    reduce_scatter x1, waiting for transfers between devices, on_device(): lax.psum_scatter(col_grad, 'dp', scatter_dimension=0, tiled=True)  25.5 us
    all_gather x1, waiting for transfers between devices, on_device(): carried_all = lax.all_gather(carried, 'dp', tiled=True)  20.3 us
    reduce_scatter x1, waiting for transfers between devices, on_device(): lax.psum_scatter(partial_value, 'tensor', scatter_dimension=1, tiled=True)  17 us
    all_gather x1, blocking collectives, on_device(): ids_all = lax.all_gather(route_ids, 'dp', tiled=True)  16.3 us
    all_gather x1, waiting for transfers between devices, on_device(): both = lax.all_gather(recv, 'tensor')  14.4 us
    reduce_sum x1, other arithmetic, on_device(): select = jnp.sum(match.astype(jnp.bfloat16), axis=2)  12.2 us
  transfers between devices with their start and end apart: 8, of which 6 were waited for; matrix products, arithmetic and copies ran while one was open for 16% of the time, Pallas kernels for 0%

profile of v1, /device:TPU:0, one launch (start us, length us, event | category | flops | bytes accessed | tf_op | source)
XLA Modules:
  0.0 306.1 jit_solution(3420084015989941428)
XLA Ops:
  9.4 16.3 %all_gather.12 = s32[512,8]{1,0:T(8,128)S(1)} all-gather(s32[128,8]{1,0:T(8,128)S(1)} %copy.23), channel_id=1, replica_groups=mesh['dp'=4,'expert'=4,'tensor'=2] {'dp'}, dimensions={0}, use_global_device_ids=true | all-gather | bytes 20480 | tf_op jit(solution)/shard_map/all_gather | solution.py:19
  26.9 12.2 %fusion.1 = bf16[1152,512]{1,0:T(8,128)(2,1)S(1)} fusion(s32[512,8]{0,1:T(8,128)S(1)} %copy.24), kind=kLoop, calls=%fused_computation.5 | loop fusion | flops 13565952 | bytes 1196032 | tf_op jit(solution)/shard_map/reduce_sum | solution.py:40
  39.1 20.3 %all-gather.3.cloned.1.call-done = bf16[512,2048]{1,0:T(8,128)(2,1)} async-done(((bf16[128,2048]{1,0:T(8,128)(2,1)}), bf16[512,2048]{1,0:T(8,128)(2,1)}) %all-gather.3.cloned.1.call-update) | async-done | bytes 2097168 | tf_op jit(solution)/shard_map/all_gather | solution.py:24
  59.4 4.4 %convolution_convert_fusion = bf16[1152,2048]{1,0:T(8,128)(2,1)S(1)} fusion(bf16[1152,512]{1,0:T(8,128)(2,1)S(1)} %fusion.1, bf16[512,2048]{1,0:T(8,128)(2,1)} %all-gather.3.cloned.1.call-done), kind=kOutput, calls=%fused_computation.6 | convolution fusion | flops 2418278400 | bytes 7995392 | tf_op jit(solution)/shard_map/dot_general | solution.py:41
  63.9 57.4 %all_to_all.42 = bf16[4,288,2048]{2,1,0:T(8,128)(2,1)} all-to-all(bf16[4,288,2048]{2,1,0:T(8,128)(2,1)S(1)} %bitcast.85), channel_id=1, replica_groups=mesh['dp'=4,'expert'=4,'tensor'=2] {'expert'}, dimensions={0} | all-to-all | bytes 9437184 | tf_op jit(solution)/shard_map/all_to_all | solution.py:45
  122.6 3.4 %all-to-all-start = ((bf16[4,128,8]{1,2,0:T(8,128)(2,1)}), bf16[4,128,8]{1,2,0:T(8,128)(2,1)S(1)}, u32[]{:S(2)}, u32[]{:S(2)}) async-start(bf16[4,128,8]{1,2,0:T(8,128)(2,1)} %stack.2), calls=%async_computation | async-start | bytes 16384 | tf_op jit(solution)/shard_map/all_to_all | solution.py:21
  126.0 14.4 %all-gather.5.cloned.1.call-done = bf16[2,1152,2048]{2,1,0:T(8,128)(2,1)} async-done(((bf16[1,1152,2048]{2,1,0:T(8,128)(2,1)}), bf16[2,1152,2048]{2,1,0:T(8,128)(2,1)}) %all-gather.5.cloned.1.call-update) | async-done | bytes 9437200 | tf_op jit(solution)/shard_map/all_gather | solution.py:47
  140.4 4.8 %fusion.9 = f32[1152,384]{0,1:T(8,128)S(1)} fusion(bf16[2,1152,2048]{2,1,0:T(8,128)(2,1)} %all-gather.5.cloned.1.call-done, bf16[1,2048,384]{2,1,0:T(8,128)(2,1)S(1)} %copy-done), kind=kOutput, calls=%fused_computation.16 | convolution fusion | flops 1811939328 | bytes 8060928 | tf_op jit(solution)/shard_map/dot_general | solution.py:53
  147.9 3.8 %fusion.17 = (f32[1152]{0:T(1024)S(1)}, bf16[1152,384]{0,1:T(8,128)(2,1)}, f32[1152,384]{0,1:T(8,128)}) fusion(f32[1152,384]{0,1:T(8,128)S(1)} %fusion.10, f32[1152,384]{0,1:T(8,128)S(1)} %fusion.9, bf16[1,384,2048]{2,1,0:T(8,128)(2,1)S(1)} %copy-done.12, bf16[2,1152,2048]{2,1,0:T(8,128)(2,1)S(1)} %copy-done.11), kind=kOutput, calls=%fused_computation.26 | convolution fusion | flops 1815919488 | bytes 12489216 | tf_op jit(solution)/shard_map/dot_general | solution.py:58
  156.2 3.9 %all-to-all-start.4 = ((bf16[4,2,144]{2,1,0:T(2,128)(2,1)}), bf16[4,2,144]{2,1,0:T(2,128)(2,1)S(1)}, u32[]{:S(2)}, u32[]{:S(2)}) async-start(bf16[4,2,144]{2,1,0:T(2,128)(2,1)} %reshape.95), calls=%async_computation.6 | async-start | bytes 8192 | tf_op jit(solution)/shard_map/all_to_all | solution.py:88
  160.1 4.7 %all-to-all-done.4 = bf16[4,2,144]{2,1,0:T(2,128)(2,1)S(1)} async-done(((bf16[4,2,144]{2,1,0:T(2,128)(2,1)}), bf16[4,2,144]{2,1,0:T(2,128)(2,1)S(1)}, u32[]{:S(2)}, u32[]{:S(2)}) %all-to-all-start.4) | async-done | bytes 2336 | tf_op jit(solution)/shard_map/all_to_all | solution.py:88
  165.0 11.9 %select_reduce_fusion = (f32[512,8]{0,1:T(8,128)}, bf16[1152]{0:T(1024)(128)(2,1)S(1)}) fusion(f32[1152]{0:T(1024)S(1)} %reshape.91, s32[512,8]{0,1:T(8,128)S(1)} %copy.24, f32[512,8]{0,1:T(8,128)S(1)} %bitcast_convert_fusion), kind=kLoop, calls=%fused_computation | loop fusion | flops 23587712 | bytes 56064 | tf_op jit(solution)/shard_map/reduce_sum | solution.py:95
  177.8 7.0 %all_to_all.43 = bf16[4,2,144]{2,1,0:T(2,128)(2,1)S(1)} all-to-all(bf16[4,2,144]{2,1,0:T(2,128)(2,1)S(1)} %reshape.97), channel_id=1, replica_groups=mesh['dp'=4,'expert'=4,'tensor'=2] {'expert'}, dimensions={0} | all-to-all | bytes 4608 | tf_op jit(solution)/shard_map/all_to_all | solution.py:46
  185.0 3.4 %multiply_convert_fusion.1 = (bf16[1152,384]{0,1:T(8,128)(2,1)S(1)}, bf16[1152,384]{0,1:T(8,128)(2,1)S(1)}) fusion(f32[1152,384]{0,1:T(8,128)} %get-tuple-element.11, f32[1152]{0:T(1024)S(1)} %reshape.90, f32[1152,384]{0,1:T(8,128)} %copy-done.5, f32[1152,384]{0,1:T(8,128)} %copy-done.6), kind=kLoop, calls=%fused_computation.29 | loop fusion | flops 6193152 | bytes 7082496 | tf_op jit(solution)/shard_map/convert_element_type | solution.py:64
  191.1 5.1 %convolution_add_fusion = f32[1152,2048]{1,0:T(8,128)} fusion(f32[1152,2048]{1,0:T(8,128)S(1)} %fusion.20, bf16[1152,384]{0,1:T(8,128)(2,1)S(1)} %get-tuple-element.9, bf16[1,2048,384]{2,1,0:T(8,128)(2,1)S(1)} %copy-done.8), kind=kOutput, calls=%fused_computation.4 | convolution fusion | flops 1814298624 | bytes 21331968 | tf_op jit(solution)/shard_map/dot_general | solution.py:80
  196.3 17.0 %reduce-scatter.4.cloned.1.call-done = f32[1152,1024]{1,0:T(8,128)} async-done(((f32[1152,2048]{1,0:T(8,128)}), f32[1152,1024]{1,0:T(8,128)}) %reduce-scatter.4.cloned.1.call-update) | async-done | bytes 4718608 | tf_op jit(solution)/shard_map/reduce_scatter | solution.py:83
  213.3 4.1 %convert_element_type.111 = bf16[1152,1024]{1,0:T(8,128)(2,1)} convert(f32[1152,1024]{1,0:T(8,128)} %reduce-scatter.4.cloned.1.call-done) | non-fusion elementwise | flops 1179648 | bytes 7077888 | tf_op jit(solution)/shard_map/convert_element_type | solution.py:83
  217.4 4.0 %all-to-all-start.3 = ((bf16[4,288,1024]{2,1,0:T(8,128)(2,1)}), bf16[4,288,1024]{2,1,0:T(8,128)(2,1)S(1)}, u32[]{:S(2)}, u32[]{:S(2)}) async-start(bf16[4,288,1024]{2,1,0:T(8,128)(2,1)} %bitcast.11), calls=%async_computation.4 | async-start | bytes 4718592 | tf_op jit(solution)/shard_map/all_to_all | solution.py:87
  222.3 27.2 %all-to-all-done.3 = bf16[4,288,1024]{2,1,0:T(8,128)(2,1)S(1)} async-done(((bf16[4,288,1024]{2,1,0:T(8,128)(2,1)}), bf16[4,288,1024]{2,1,0:T(8,128)(2,1)S(1)}, u32[]{:S(2)}, u32[]{:S(2)}) %all-to-all-start.3) | async-done | bytes 2359328 | tf_op jit(solution)/shard_map/all_to_all | solution.py:87
  249.5 4.1 %fusion.38 = f32[512,1024]{1,0:T(8,128)} fusion(bf16[1152,512]{1,0:T(8,128)(2,1)} %copy-done.2, bf16[1152,1024]{1,0:T(8,128)(2,1)S(1)} %bitcast.84), kind=kOutput, calls=%fused_computation.53 | convolution fusion | flops 1207959552 | bytes 5636096 | tf_op jit(solution)/shard_map/dot_general | solution.py:89
  254.7 5.8 %fusion.14 = bf16[1,384,2048]{2,1,0:T(8,128)(2,1)} fusion(bf16[2,1152,2048]{2,1,0:T(8,128)(2,1)} %all-gather.5.cloned.1.call-done, bf16[1152,384]{0,1:T(8,128)(2,1)S(1)} %copy-done.13, f32[1152]{0:T(1024)S(1)} %reshape.90), kind=kOutput, calls=%fused_computation.21 | convolution fusion | flops 1814052864 | bytes 7180800 | tf_op jit(solution)/shard_map/dot_general | solution.py:75
  260.6 6.4 %fusion.15 = bf16[1,2048,384]{2,1,0:T(8,128)(2,1)} fusion(bf16[1152,384]{0,1:T(8,128)(2,1)S(1)} %get-tuple-element.9, bf16[2,1152,2048]{2,1,0:T(8,128)(2,1)} %all-gather.5.cloned.1.call-done), kind=kOutput, calls=%fused_computation.22 | convolution fusion | flops 1812725760 | bytes 7176192 | tf_op jit(solution)/shard_map/dot_general | solution.py:71
  267.0 3.9 %fusion.16 = bf16[1,2048,384]{2,1,0:T(8,128)(2,1)} fusion(bf16[1152,384]{0,1:T(8,128)(2,1)S(1)} %copy-done.4, bf16[2,1152,2048]{2,1,0:T(8,128)(2,1)S(1)} %bitcast.89), kind=kOutput, calls=%fused_computation.23 | convolution fusion | flops 1812725760 | bytes 7176192 | tf_op jit(solution)/shard_map/dot_general | solution.py:68
  272.2 25.5 %reduce-scatter.6.cloned.1.call-done = f32[128,1024]{1,0:T(8,128)} async-done(((f32[512,1024]{1,0:T(8,128)}), f32[128,1024]{1,0:T(8,128)}) %reduce-scatter.6.cloned.1.call-update) | async-done | bytes 524304 | tf_op jit(solution)/shard_map/reduce_scatter | solution.py:92
  (78 shorter events, 20.8 us)
Async XLA Ops:
  7.2 133.3 %copy-start = (bf16[1,2048,384]{2,1,0:T(8,128)(2,1)S(1)}, bf16[1,2048,384]{2,1,0:T(8,128)(2,1)}, u32[]{:S(2)}) copy-start(bf16[1,2048,384]{2,1,0:T(8,128)(2,1)} %param.11) | copy-start | bytes 4718596
  7.2 2.1 copy-start.9
  7.2 52.2 %all-gather.3.cloned.1.call-start = ((), (), s32[]{:S(2)}) async-start(), calls=%async_computation.8 | async-start | bytes 2621440 | tf_op jit(solution)/shard_map/all_gather | solution.py:24
  9.3 131.1 %all-gather.5.cloned.1.call-start = ((), (), s32[]{:S(2)}) async-start(), calls=%async_computation.9 | async-start | bytes 14155776 | tf_op jit(solution)/shard_map/all_gather | solution.py:47
  39.1 24.7 %copy-start.2 = (bf16[1152,512]{1,0:T(8,128)(2,1)}, bf16[1152,512]{1,0:T(8,128)(2,1)S(1)}, u32[]{:S(2)}) copy-start(bf16[1152,512]{1,0:T(8,128)(2,1)S(1)} %fusion.1) | copy-start | bytes 3538948
  122.6 33.7 %all-to-all-start = ((bf16[4,128,8]{1,2,0:T(8,128)(2,1)}), bf16[4,128,8]{1,2,0:T(8,128)(2,1)S(1)}, u32[]{:S(2)}, u32[]{:S(2)}) async-start(bf16[4,128,8]{1,2,0:T(8,128)(2,1)} %stack.2), calls=%async_computation | async-start | bytes 16384 | tf_op jit(solution)/shard_map/all_to_all | solution.py:21
  126.0 19.2 %copy-start.7 = (bf16[1,2048,384]{2,1,0:T(8,128)(2,1)S(1)}, bf16[1,2048,384]{2,1,0:T(8,128)(2,1)}, u32[]{:S(2)}) copy-start(bf16[1,2048,384]{2,1,0:T(8,128)(2,1)} %param.12) | copy-start | bytes 4718596
  140.4 5.1 %copy-start.11 = (bf16[2,1152,2048]{2,1,0:T(8,128)(2,1)S(1)}, bf16[2,1152,2048]{2,1,0:T(8,128)(2,1)}, u32[]{:S(2)}) copy-start(bf16[2,1152,2048]{2,1,0:T(8,128)(2,1)} %all-gather.5.cloned.1.call-done) | copy-start | bytes 28311556
  145.5 2.4 copy-start.5
  145.5 2.4 copy-start.12
  147.9 3.9 %copy-start.6 = (f32[1152,384]{0,1:T(8,128)}, f32[1152,384]{0,1:T(8,128)S(1)}, u32[]{:S(2)}) copy-start(f32[1152,384]{0,1:T(8,128)S(1)} %fusion.10) | copy-start | bytes 5308420
  156.2 8.6 %all-to-all-start.4 = ((bf16[4,2,144]{2,1,0:T(2,128)(2,1)}), bf16[4,2,144]{2,1,0:T(2,128)(2,1)S(1)}, u32[]{:S(2)}, u32[]{:S(2)}) async-start(bf16[4,2,144]{2,1,0:T(2,128)(2,1)} %reshape.95), calls=%async_computation.6 | async-start | bytes 8192 | tf_op jit(solution)/shard_map/all_to_all | solution.py:88
  160.1 53.2 %reduce-scatter.4.cloned.1.call-start = ((), (), s32[]{:S(2)}) async-start(), calls=%async_computation.10 | async-start | bytes 14155776 | tf_op jit(solution)/shard_map/reduce_scatter | solution.py:83
  188.4 2.7 copy-start.3
  188.4 2.7 copy-start.8
  217.4 32.1 %all-to-all-start.3 = ((bf16[4,288,1024]{2,1,0:T(8,128)(2,1)}), bf16[4,288,1024]{2,1,0:T(8,128)(2,1)S(1)}, u32[]{:S(2)}, u32[]{:S(2)}) async-start(bf16[4,288,1024]{2,1,0:T(8,128)(2,1)} %bitcast.11), calls=%async_computation.4 | async-start | bytes 4718592 | tf_op jit(solution)/shard_map/all_to_all | solution.py:87
  221.4 49.5 %reduce-scatter.8.cloned.1.call-start = ((), (), s32[]{:S(2)}) async-start(), calls=%async_computation.12 | async-start | bytes 20480 | tf_op jit(solution)/shard_map/reduce_scatter | solution.py:96
  222.0 75.8 %reduce-scatter.6.cloned.1.call-start = ((), (), s32[]{:S(2)}) async-start(), calls=%async_computation.11 | async-start | bytes 2621440 | tf_op jit(solution)/shard_map/reduce_scatter | solution.py:92
  253.6 1.2 copy-start.13
  254.7 12.3 %slice-start = ((s8[9437184]{0:T(1024)(128)(4,1)}), s8[4194304]{0:T(1024)(128)(4,1)S(1)}, s32[]{:S(2)}) async-start(s8[9437184]{0:T(1024)(128)(4,1)} %bitcast.88), calls=%async_computation.13 | async-start | bytes 8388608
  254.7 12.3 %slice-start.1 = ((s8[9437184]{0:T(1024)(128)(4,1)}), s8[4194304]{0:T(1024)(128)(4,1)S(1)}, s32[]{:S(2)}) async-start(s8[9437184]{0:T(1024)(128)(4,1)} %bitcast.88), calls=%async_computation.14 | async-start | bytes 8388608
  260.6 6.4 %copy-start.4 = (bf16[1152,384]{0,1:T(8,128)(2,1)S(1)}, bf16[1152,384]{0,1:T(8,128)(2,1)}, u32[]{:S(2)}) copy-start(bf16[1152,384]{0,1:T(8,128)(2,1)} %copy-done.3) | copy-start | bytes 2654212
  260.6 6.4 %slice-start.2 = ((s8[9437184]{0:T(1024)(128)(4,1)}), s8[1048576]{0:T(1024)(128)(4,1)S(1)}, s32[]{:S(2)}) async-start(s8[9437184]{0:T(1024)(128)(4,1)} %bitcast.88), calls=%async_computation.15 | async-start | bytes 2097152
  267.0 32.5 %copy-start.1 = (bf16[1,2048,384]{2,1,0:T(8,128)(2,1)S(1)}, bf16[1,2048,384]{2,1,0:T(8,128)(2,1)}, u32[]{:S(2)}) copy-start(bf16[1,2048,384]{2,1,0:T(8,128)(2,1)} %param.11) | copy-start | bytes 4718596
  (1 other events, 0.7 us)
Sparse Core Ops, SparseCore 0:
  10.2 49.2 all-gather.2
  121.4 18.9 all-gather.4
  196.4 16.8 reduce-scatter.3
  224.8 20.3 reduce-scatter.7
  253.7 44.0 reduce-scatter.5
